TPU v7x, 256 devices: a whole 4x4x8 slice. The times are simulated.
256 devices in a mesh: dp: 4 (over y), expert: 64 (over x, z, core).
Axes of the slice: x: 4, y: 4, z: 8, core: 2. Of those that a mesh axis runs over, the one named last changes fastest.
Arguments:
- hidden: bfloat16 [32768, 2, 1024], P(('dp', 'expert')), may hold values from -6 to 6
- routes: int32 [32768, 2], P(('dp', 'expert')), may hold values from 0 to 63, all different within a row; in each aligned block of 128 rows (0 to 127, 128 to 255, ...) at most 8 rows name the same one
- gates: float32 [32768, 2], P(('dp', 'expert')), may hold values from 0.1 to 1
- cotangent: bfloat16 [32768, 7168], P(('dp', 'expert')), may hold values from -1.796875 to 1.796875
- weight: bfloat16 [64, 1024, 7168], P('expert', None, 'dp'), may hold values from -0.0625 to 0.0625
Outputs:
- grad_hidden: bfloat16 [32768, 2, 1024], P(('dp', 'expert'))
- grad_gates: float32 [32768, 2], P(('dp', 'expert'))
- grad_weight: bfloat16 [64, 1024, 7168], P('expert', None, 'dp')
Inputs may be any that keep to these rules, and one draw needn't show every extreme that they name: `routes`: each row names 2 different experts; in each aligned block of 128 rows (the rows of one device) no expert is named by more than 8 rows, a bound that some block reaches.
All inputs are finite; a program needn't handle non-finite values.
Results may differ from a plain program's by a relative error of at most 0.0049.
Values may be sent and summed in bfloat16 or wider, within the bound.
No kernel may reach another device: no remote copies, remote signals or barrier semaphores. Data moves between devices by JAX's collectives and lax.ppermute only.
A program may use at most 128 MiB of HBM per device.

v0:
```python
import jax
import jax.numpy as jnp
from jax import lax
from jax.sharding import PartitionSpec as P


def per_device(hidden, routes, gates, cotangent, weight):
    local_tokens, top_count, hidden_width = hidden.shape
    columns = lax.axis_size("expert")
    capacity = min(local_tokens, 2 * local_tokens * top_count // columns)
    slot_count = local_tokens * top_count
    flat_experts = routes.reshape(slot_count)
    one_hot = (flat_experts[:, None] == jnp.arange(columns, dtype=jnp.int32)[None, :]).astype(
        jnp.int32
    )
    earlier = jnp.cumsum(one_hot, axis=0) - one_hot
    position = jnp.sum(earlier * one_hot, axis=1)
    destination = flat_experts * capacity + position
    slot_of = (
        jnp.full((columns * capacity,), slot_count, jnp.int32)
        .at[destination]
        .set(jnp.arange(slot_count, dtype=jnp.int32))
    )
    scaled = (
        (gates[:, :, None] * hidden.astype(jnp.float32))
        .astype(jnp.bfloat16)
        .reshape(slot_count, hidden_width)
    )
    scaled = jnp.concatenate([scaled, jnp.zeros((1, hidden_width), jnp.bfloat16)], axis=0)
    cot_pad = jnp.concatenate([cotangent, jnp.zeros((1, cotangent.shape[1]), jnp.bfloat16)], axis=0)
    send_rows = scaled[slot_of].reshape(columns, capacity, hidden_width)
    send_cot = cot_pad[slot_of // top_count].reshape(columns, capacity, cotangent.shape[1])
    got_rows, got_cot = (
        lax.all_to_all(send_rows, "expert", split_axis=0, concat_axis=0, tiled=True),
        lax.all_to_all(send_cot, "expert", split_axis=0, concat_axis=0, tiled=True),
    )
    cot_quarter = lax.all_to_all(got_cot[None], "dp", split_axis=3, concat_axis=0, tiled=True)
    rows_all = lax.all_gather(got_rows[None], "dp", axis=0, tiled=True)
    matrix = weight[0]
    partial_back = jnp.einsum(
        "bscd,fd->bscf", cot_quarter, matrix, preferred_element_type=jnp.float32
    )
    summed = lax.psum_scatter(partial_back, "dp", scatter_dimension=0, tiled=True)
    grad_matrix = jnp.einsum(
        "bscf,bscd->fd", rows_all, cot_quarter, preferred_element_type=jnp.float32
    )
    returned = lax.all_to_all(summed[0], "expert", split_axis=0, concat_axis=0, tiled=True)
    back = returned.reshape(columns * capacity, hidden_width)[destination]
    grad_hidden = (
        (gates.reshape(slot_count)[:, None] * back)
        .astype(jnp.bfloat16)
        .reshape(local_tokens, top_count, hidden_width)
    )
    grad_gates = jnp.sum(
        hidden.reshape(slot_count, hidden_width).astype(jnp.float32) * back, axis=1
    ).reshape(local_tokens, top_count)
    return (grad_hidden, grad_gates, grad_matrix.astype(jnp.bfloat16)[None])


def solution(mesh):
    placed = (
        P(("dp", "expert"), None, None),
        P(("dp", "expert"), None),
        P(("dp", "expert"), None),
        P(("dp", "expert"), None),
        P("expert", None, "dp"),
    )
    return jax.shard_map(
        per_device,
        mesh=mesh,
        in_specs=placed,
        out_specs=(
            P(("dp", "expert"), None, None),
            P(("dp", "expert"), None),
            P("expert", None, "dp"),
        ),
        check_vma=False,
    )
```

profile of v0, /device:TPU:1, one launch (start us, length us, event | category | flops | bytes accessed | tf_op | source)
XLA Modules:
  0.0 613.7 jit_solution(7053803963562707793)
XLA Ops:
  7.2 0.8 copy.29
  8.3 0.7 broadcast_multiply_fusion
  9.0 0.6 reduce-window.6
  10.2 1.4 scatter_custom_fusion
  11.6 1.7 concatenate.6
  13.3 7.1 %gather_fusion = bf16[512,7168]{1,0:T(8,128)(2,1)} fusion(bf16[129,7168]{1,0:T(8,128)(2,1)S(1)} %concatenate.6, s32[1024]{0:T(1024)S(1)} %get-tuple-element.15), kind=kCustom, calls=%fused_computation | custom fusion | bytes 14682112 | tf_op jit(solution)/shard_map/gather | solution.py:32
  20.4 176.4 %all_to_all.33 = bf16[64,8,7168]{2,1,0:T(8,128)(2,1)} all-to-all(bf16[64,8,7168]{2,1,0:T(8,128)(2,1)} %bitcast.60), channel_id=1, replica_groups=mesh['dp'=4,'expert'=64] {'expert'}, dimensions={0} | all-to-all | bytes 14680064 | tf_op jit(solution)/shard_map/all_to_all | solution.py:35
  196.8 19.3 %copy.32 = bf16[1,64,8,7168]{1,2,0,3:T(8,128)(2,1)} copy(bf16[1,64,8,7168]{3,2,1,0:T(8,128)(2,1)} %bitcast.61) | data formatting | bytes 14680064 | tf_op jit(solution)/shard_map/broadcast_in_dim | solution.py:37
  216.1 14.8 %reshape.123 = bf16[4,2,458752]{2,1,0:T(2,128)(2,1)} reshape(bf16[7168,1,8,64]{3,2,1,0:T(8,128)(2,1)} %bitcast.57) | data formatting | bytes 14680064
  230.9 90.1 %all_to_all.34 = bf16[4,2,458752]{2,1,0:T(2,128)(2,1)} all-to-all(bf16[4,2,458752]{2,1,0:T(2,128)(2,1)} %reshape.123), channel_id=1, replica_groups=mesh['dp'=4,'expert'=64] {'dp'}, dimensions={0} | all-to-all | bytes 14680064 | tf_op jit(solution)/shard_map/all_to_all | solution.py:37
  321.0 14.3 %reshape.124 = bf16[7168,1,8,64]{3,2,1,0:T(8,128)(2,1)} reshape(bf16[4,2,458752]{2,1,0:T(2,128)(2,1)} %all_to_all.34) | data formatting | bytes 14680064
  335.3 17.7 %copy.34 = bf16[1,64,8,4,1792]{4,2,1,3,0:T(8,128)(2,1)} copy(bf16[1,64,8,4,1792]{1,2,4,3,0:T(8,128)(2,1)} %bitcast.58) | data formatting | bytes 14680064 | tf_op jit(solution)/shard_map/all_to_all | solution.py:37
  353.1 13.2 %fusion.2 = f32[4,64,8,1024]{3,2,1,0:T(8,128)} fusion(bf16[1,64,8,4,1792]{4,2,1,3,0:T(8,128)(2,1)} %copy.34, bf16[1,1024,1792]{2,1,0:T(8,128)(2,1)} %param.9), kind=kOutput, calls=%fused_computation.7 | convolution fusion | flops 7516192768 | bytes 19398656 | tf_op jit(solution)/shard_map/bscd,fd->bscf/dot_general | solution.py:40
  366.3 78.2 %reduce-scatter.2.cloned.1.call-done = f32[1,64,8,1024]{3,2,1,0:T(8,128)} async-done(((f32[4,64,8,1024]{3,2,1,0:T(8,128)}), f32[1,64,8,1024]{3,2,1,0:T(8,128)}) %reduce-scatter.2.cloned.1.call-update) | async-done | bytes 2097168 | tf_op jit(solution)/shard_map/reduce_scatter | solution.py:43
  444.5 10.7 %all-to-all-start.2 = ((f32[64,8,1024]{2,1,0:T(8,128)}), f32[64,8,1024]{2,1,0:T(8,128)S(1)}, u32[]{:S(2)}, u32[]{:S(2)}) async-start(f32[64,8,1024]{2,1,0:T(8,128)} %bitcast.63), calls=%async_computation.3 | async-start | bytes 4194304 | tf_op jit(solution)/shard_map/all_to_all | solution.py:47
  455.4 51.0 %all-to-all-done.2 = f32[64,8,1024]{2,1,0:T(8,128)S(1)} async-done(((f32[64,8,1024]{2,1,0:T(8,128)}), f32[64,8,1024]{2,1,0:T(8,128)S(1)}, u32[]{:S(2)}, u32[]{:S(2)}) %all-to-all-start.2) | async-done | bytes 2097184 | tf_op jit(solution)/shard_map/all_to_all | solution.py:47
  506.4 1.1 gather_fusion.1
  507.5 0.6 gather.13
  508.1 3.0 fusion.10
  511.4 2.1 gather_fusion.2
  513.5 34.3 %all_to_all.35 = bf16[64,8,1024]{2,1,0:T(8,128)(2,1)} all-to-all(bf16[64,8,1024]{2,1,0:T(8,128)(2,1)S(1)} %bitcast.62), channel_id=1, replica_groups=mesh['dp'=4,'expert'=64] {'expert'}, dimensions={0} | all-to-all | bytes 2097152 | tf_op jit(solution)/shard_map/all_to_all | solution.py:34
  547.8 0.6 copy.35
  548.4 45.4 %all-gather.3.cloned.1.call-done = bf16[256,8,1024]{2,1,0:T(8,128)(2,1)} async-done(((bf16[64,8,1024]{2,1,0:T(8,128)(2,1)}), bf16[256,8,1024]{2,1,0:T(8,128)(2,1)}) %all-gather.3.cloned.1.call-update) | async-done | bytes 4194320 | tf_op jit(solution)/shard_map/all_gather | solution.py:38
  593.8 13.0 %fusion.7 = bf16[1,1024,1792]{2,1,0:T(8,128)(2,1)} fusion(bf16[4,64,8,1024]{3,2,1,0:T(8,128)(2,1)} %bitcast.67, bf16[1,64,8,4,1792]{4,2,1,3,0:T(8,128)(2,1)} %copy.34), kind=kOutput, calls=%fused_computation.10 | convolution fusion | flops 7518027776 | bytes 15204352 | tf_op jit(solution)/shard_map/bscf,bscd->fd/dot_general | solution.py:44
  (23 shorter events, 1.4 us)
Async XLA Ops:
  7.2 437.3 %reduce-scatter.2.cloned.1.call-start = ((), (), s32[]{:S(2)}) async-start(), calls=%async_computation.5 | async-start | bytes 10485760 | tf_op jit(solution)/shard_map/reduce_scatter | solution.py:43
  366.2 89.0 %copy-start = (f32[128,2]{0,1:T(2,128)S(1)}, f32[128,2]{0,1:T(2,128)}, u32[]{:S(2)}) copy-start(f32[128,2]{0,1:T(2,128)} %param.7) | copy-start | bytes 3076
  444.5 61.9 %all-to-all-start.2 = ((f32[64,8,1024]{2,1,0:T(8,128)}), f32[64,8,1024]{2,1,0:T(8,128)S(1)}, u32[]{:S(2)}, u32[]{:S(2)}) async-start(f32[64,8,1024]{2,1,0:T(8,128)} %bitcast.63), calls=%async_computation.3 | async-start | bytes 4194304 | tf_op jit(solution)/shard_map/all_to_all | solution.py:47
  455.2 138.6 %all-gather.3.cloned.1.call-start = ((), (), s32[]{:S(2)}) async-start(), calls=%async_computation.6 | async-start | bytes 5242880 | tf_op jit(solution)/shard_map/all_gather | solution.py:38
Sparse Core Ops, SparseCore 0:
  366.4 78.0 reduce-scatter.1
  547.9 45.8 all-gather.2
where the time goes:
time: 615 us; the launch traced here: 614 us
  blocking collectives  301 us (49%)
  waiting for transfers between devices  175 us (28%)
  local copies, waits for them, and re-layouts  82.5 us (13%)
  matrix products  26.2 us (4%)
  between operations  14.2 us (2%)
  starting transfers between devices  10.8 us (2%)
    all_to_all x1, blocking collectives, per_device(): lax.all_to_all(send_cot, 'expert', split_axis=0, concat_axis=0, tiled=True)  176 us
    all_to_all x1, blocking collectives, per_device(): lax.all_to_all(got_cot[None], 'dp', split_axis=3, concat_axis=0, tiled=True)  90.1 us
    reduce_scatter x1, waiting for transfers between devices, per_device(): lax.psum_scatter(partial_back, 'dp', scatter_dimension=0, tiled=True)  78.2 us
    all_to_all x1, waiting for transfers between devices, per_device(): lax.all_to_all(summed[0], 'expert', split_axis=0, concat_axis=0, tiled=True)  51 us
    all_gather x1, waiting for transfers between devices, per_device(): rows_all = lax.all_gather(got_rows[None], 'dp', axis=0, tiled=True)  45.4 us
    all_to_all x1, blocking collectives, per_device(): lax.all_to_all(send_rows, 'expert', split_axis=0, concat_axis=0, tiled=True)  34.3 us
    unnamed x7, local copies, waits for them, and re-layouts  30.6 us
    broadcast_in_dim x1, local copies, waits for them, and re-layouts, per_device(): got_cot[None]  19.3 us
  transfers between devices with their start and end apart: 3, of which 3 were waited for; matrix products, arithmetic and copies ran while one was open for 0% of the time, Pallas kernels for 0%

commit v1 on v0

--- a/solution.py
+++ b/solution.py
@@ -34,7 +34,11 @@
         lax.all_to_all(send_rows, "expert", split_axis=0, concat_axis=0, tiled=True),
         lax.all_to_all(send_cot, "expert", split_axis=0, concat_axis=0, tiled=True),
     )
-    cot_quarter = lax.all_to_all(got_cot[None], "dp", split_axis=3, concat_axis=0, tiled=True)
+    part = got_cot[None]
+    devices = lax.axis_size("dp")
+    blocks = jnp.stack(jnp.split(part, devices, axis=3), axis=0)
+    blocks = lax.all_to_all(blocks, "dp", split_axis=0, concat_axis=0)
+    cot_quarter = jnp.concatenate(blocks, axis=0)
     rows_all = lax.all_gather(got_rows[None], "dp", axis=0, tiled=True)
     matrix = weight[0]
     partial_back = jnp.einsum(

time: 615 us -> 546 us (0.89)
  local copies, waits for them, and re-layouts: 82.5 us -> 19.9 us
    unnamed x7 -> x9, local copies, waits for them, and re-layouts: 30.6 us -> 4.55 us
    broadcast_in_dim x1 -> x0, local copies, waits for them, and re-layouts: 19.3 us -> none  [per_device(): got_cot[None]]
    all_to_all x1 -> x0, local copies, waits for them, and re-layouts: 17.7 us -> none  [per_device(): lax.all_to_all(got_cot[None], 'dp', split_axis=3, concat_axis=0, tiled=True)]
where the time goes in v1:
time: 546 us
  blocking collectives  297 us (54%)
  waiting for transfers between devices  175 us (32%)
  matrix products  23 us (4%)
  local copies, waits for them, and re-layouts  19.9 us (4%)
  between operations  14.2 us (3%)
  starting transfers between devices  11 us (2%)
  other arithmetic  5.51 us (1%)
    all_to_all x1, blocking collectives, per_device(): lax.all_to_all(send_cot, 'expert', split_axis=0, concat_axis=0, tiled=True)  176 us
    all_to_all x1, blocking collectives, per_device(): blocks = lax.all_to_all(blocks, 'dp', split_axis=0, concat_axis=0)  86.6 us
    reduce_scatter x1, waiting for transfers between devices, per_device(): lax.psum_scatter(partial_back, 'dp', scatter_dimension=0, tiled=True)  78.7 us
    all_to_all x1, waiting for transfers between devices, per_device(): lax.all_to_all(summed[0], 'expert', split_axis=0, concat_axis=0, tiled=True)  50.8 us
    all_gather x1, waiting for transfers between devices, per_device(): rows_all = lax.all_gather(got_rows[None], 'dp', axis=0, tiled=True)  45.4 us
    all_to_all x1, blocking collectives, per_device(): lax.all_to_all(send_rows, 'expert', split_axis=0, concat_axis=0, tiled=True)  34.3 us
    dot_general x1, matrix products, per_device(): jnp.einsum('bscf,bscd->fd', rows_all, cot_quarter, preferred_element_type...  13 us
  transfers between devices with their start and end apart: 3, of which 3 were waited for; matrix products, arithmetic and copies ran while one was open for 0% of the time, Pallas kernels for 0%

profile of v1, /device:TPU:1, one launch (start us, length us, event | category | flops | bytes accessed | tf_op | source)
XLA Modules:
  0.0 545.7 jit_solution(17191187257097761906)
XLA Ops:
  7.2 0.8 copy.25
  8.3 0.7 broadcast_multiply_fusion
  9.0 0.6 reduce-window.6
  10.2 1.4 scatter_custom_fusion
  11.6 1.7 concatenate.6
  13.3 7.1 %gather_fusion = bf16[512,7168]{1,0:T(8,128)(2,1)} fusion(bf16[129,7168]{1,0:T(8,128)(2,1)S(1)} %concatenate.6, s32[1024]{0:T(1024)S(1)} %get-tuple-element.16), kind=kCustom, calls=%fused_computation | custom fusion | bytes 14682112 | tf_op jit(solution)/shard_map/gather | solution.py:32
  20.4 176.3 %all_to_all.20 = bf16[64,8,7168]{2,1,0:T(8,128)(2,1)S(1)} all-to-all(bf16[64,8,7168]{2,1,0:T(8,128)(2,1)} %bitcast.61), channel_id=1, replica_groups=mesh['dp'=4,'expert'=64] {'expert'}, dimensions={0} | all-to-all | bytes 14680064 | tf_op jit(solution)/shard_map/all_to_all | solution.py:35
  196.7 0.5 slice_bitcast_fusion.3
  197.2 1.0 pad_maximum_fusion
  198.2 86.6 %all_to_all.21 = bf16[4,1,64,8,1792]{4,3,2,1,0:T(8,128)(2,1)S(1)} all-to-all(bf16[4,1,64,8,1792]{4,3,2,1,0:T(8,128)(2,1)S(1)} %pad_maximum_fusion), channel_id=1, replica_groups=mesh['dp'=4,'expert'=64] {'dp'}, dimensions={0} | all-to-all | bytes 14680064 | tf_op jit(solution)/shard_map/all_to_all | solution.py:40
  284.8 3.0 copy-done
  287.8 10.0 %fusion.2 = f32[4,64,8,1024]{3,2,1,0:T(8,128)} fusion(bf16[4,1,64,8,1792]{4,3,2,1,0:T(8,128)(2,1)S(1)} %all_to_all.21, bf16[1,1024,1792]{2,1,0:T(8,128)(2,1)S(1)} %copy-done.2), kind=kOutput, calls=%fused_computation.8 | convolution fusion | flops 7516192768 | bytes 19398656 | tf_op jit(solution)/shard_map/bscd,fd->bscf/dot_general | solution.py:44
  297.8 78.7 %reduce-scatter.2.cloned.1.call-done = f32[1,64,8,1024]{3,2,1,0:T(8,128)} async-done(((f32[4,64,8,1024]{3,2,1,0:T(8,128)}), f32[1,64,8,1024]{3,2,1,0:T(8,128)}) %reduce-scatter.2.cloned.1.call-update) | async-done | bytes 2097168 | tf_op jit(solution)/shard_map/reduce_scatter | solution.py:47
  376.5 10.7 %all-to-all-start.2 = ((f32[64,8,1024]{2,1,0:T(8,128)}), f32[64,8,1024]{2,1,0:T(8,128)S(1)}, u32[]{:S(2)}, u32[]{:S(2)}) async-start(f32[64,8,1024]{2,1,0:T(8,128)} %bitcast.64), calls=%async_computation.3 | async-start | bytes 4194304 | tf_op jit(solution)/shard_map/all_to_all | solution.py:51
  387.2 0.2 all-gather.3.cloned.1.call-start
  387.6 50.8 %all-to-all-done.2 = f32[64,8,1024]{2,1,0:T(8,128)S(1)} async-done(((f32[64,8,1024]{2,1,0:T(8,128)}), f32[64,8,1024]{2,1,0:T(8,128)S(1)}, u32[]{:S(2)}, u32[]{:S(2)}) %all-to-all-start.2) | async-done | bytes 2097184 | tf_op jit(solution)/shard_map/all_to_all | solution.py:51
  438.4 1.1 gather_fusion.1
  439.5 0.6 gather.13
  440.1 3.0 fusion.10
  443.4 2.1 gather_fusion.2
  445.5 34.3 %all_to_all.22 = bf16[64,8,1024]{2,1,0:T(8,128)(2,1)} all-to-all(bf16[64,8,1024]{2,1,0:T(8,128)(2,1)S(1)} %bitcast.63), channel_id=1, replica_groups=mesh['dp'=4,'expert'=64] {'expert'}, dimensions={0} | all-to-all | bytes 2097152 | tf_op jit(solution)/shard_map/all_to_all | solution.py:34
  479.8 0.6 copy.28
  480.4 45.4 %all-gather.3.cloned.1.call-done = bf16[256,8,1024]{2,1,0:T(8,128)(2,1)} async-done(((bf16[64,8,1024]{2,1,0:T(8,128)(2,1)}), bf16[256,8,1024]{2,1,0:T(8,128)(2,1)}) %all-gather.3.cloned.1.call-update) | async-done | bytes 4194320 | tf_op jit(solution)/shard_map/all_gather | solution.py:42
  525.8 13.0 %fusion.7 = bf16[1,1024,1792]{2,1,0:T(8,128)(2,1)} fusion(bf16[4,64,8,1024]{3,2,1,0:T(8,128)(2,1)} %bitcast.68, bf16[4,1,64,8,1792]{4,3,2,1,0:T(8,128)(2,1)} %copy-done), kind=kOutput, calls=%fused_computation.11 | convolution fusion | flops 7518027776 | bytes 15204352 | tf_op jit(solution)/shard_map/bscf,bscd->fd/dot_general | solution.py:48
  (25 shorter events, 1.3 us)
Async XLA Ops:
  7.2 369.3 %reduce-scatter.2.cloned.1.call-start = ((), (), s32[]{:S(2)}) async-start(), calls=%async_computation.5 | async-start | bytes 10485760 | tf_op jit(solution)/shard_map/reduce_scatter | solution.py:47
  198.2 89.6 %copy-start.2 = (bf16[1,1024,1792]{2,1,0:T(8,128)(2,1)S(1)}, bf16[1,1024,1792]{2,1,0:T(8,128)(2,1)}, u32[]{:S(2)}) copy-start(bf16[1,1024,1792]{2,1,0:T(8,128)(2,1)} %param.9) | copy-start | bytes 11010052
  284.8 3.0 copy-start
  297.8 89.7 %copy-start.1 = (f32[128,2]{0,1:T(2,128)S(1)}, f32[128,2]{0,1:T(2,128)}, u32[]{:S(2)}) copy-start(f32[128,2]{0,1:T(2,128)} %param.7) | copy-start | bytes 3076
  376.5 61.9 %all-to-all-start.2 = ((f32[64,8,1024]{2,1,0:T(8,128)}), f32[64,8,1024]{2,1,0:T(8,128)S(1)}, u32[]{:S(2)}, u32[]{:S(2)}) async-start(f32[64,8,1024]{2,1,0:T(8,128)} %bitcast.64), calls=%async_computation.3 | async-start | bytes 4194304 | tf_op jit(solution)/shard_map/all_to_all | solution.py:51
  387.2 138.6 %all-gather.3.cloned.1.call-start = ((), (), s32[]{:S(2)}) async-start(), calls=%async_computation.6 | async-start | bytes 5242880 | tf_op jit(solution)/shard_map/all_gather | solution.py:42
Sparse Core Ops, SparseCore 0:
  297.9 78.5 reduce-scatter.1
  479.9 45.8 all-gather.2
